TPU v7x, 32 devices: a whole 2x2x4 slice. The times are simulated.
32 devices in a mesh: seq: 8 (over z, y), tp: 4 (over x, core).
Axes of the slice: x: 2, y: 2, z: 4, core: 2. Of those that a mesh axis runs over, the one named last changes fastest.
Arguments:
- new_query: bfloat16 [8, 3584], P('seq', 'tp'), may hold values from -360 to 360
- new_key: bfloat16 [8, 512], P('seq', 'tp'), may hold values from -6 to 6
- new_value: bfloat16 [8, 512], P('seq', 'tp'), may hold values from -6 to 6
- cache_keys: bfloat16 [8, 4096, 512], P('seq', None, 'tp'), may hold values from -6 to 6
- cache_values: bfloat16 [8, 4096, 512], P('seq', None, 'tp'), may hold values from -6 to 6
- cache_length: int32 [8], P('seq'), may hold values from 1 to 4096, 16384 in all
- dealing: int32 [8], replicated, may hold values from 0 to 7, each once
- out_weight: bfloat16 [3584, 3584], P('tp', 'seq'), may hold values from -0.09375 to 0.09375
- stretch_query: bfloat16 [3, 256, 3584], P(None, 'seq', 'tp'), may hold values from -360 to 360
- stretch_key: bfloat16 [3, 256, 512], P(None, 'seq', 'tp'), may hold values from -6 to 6
- stretch_value: bfloat16 [3, 256, 512], P(None, 'seq', 'tp'), may hold values from -6 to 6
- prior_keys: bfloat16 [3, 8192, 512], P(None, 'seq', 'tp'), may hold values from -6 to 6
- prior_values: bfloat16 [3, 8192, 512], P(None, 'seq', 'tp'), may hold values from -6 to 6
- stretch_start: int32 [3], replicated, may hold values from 1 to 8192, 16384 in all
Outputs:
- decode_mixed: bfloat16 [8, 3584], P('tp', 'seq')
- stretch_out: bfloat16 [3, 256, 3584], P(None, 'seq', 'tp')
Inputs may be any that keep to these rules, and one draw needn't show every extreme that they name: dealing[a] is the cache slot of the decode request that arrives a-th; every slot appears once. `cache_length`: cached positions in use of each decode slot; one slot is full. `stretch_start`: cached positions of each stretch's request that precede the stretch; one request's cache is full.
All inputs are finite; a program needn't handle non-finite values. No bound on the sum of `cache_length` on one device may be relied on, other than what follows from the above.
Results may differ from a plain program's by a relative error of at most 0.0051.
Values may be sent and summed in bfloat16 or wider, within the bound.
No kernel may reach another device: no remote copies, remote signals or barrier semaphores. Data moves between devices by JAX's collectives and lax.ppermute only.
A program may use at most 64 MiB of HBM per device.

v0:
```python
import math
import jax
import jax.numpy as jnp
from jax import lax
from jax.sharding import PartitionSpec as P

NEG_FILL = -1e30


def partial_attend(queries, keys, values, visible):
    factor = 1.0 / math.sqrt(queries.shape[-1])
    scores = jnp.dot(queries, keys.T, preferred_element_type=jnp.float32) * factor
    scores = jnp.where(visible, scores, NEG_FILL)
    row_top = jnp.max(scores, axis=1)
    weights = jnp.where(visible, jnp.exp(scores - row_top[:, None]), 0.0)
    weight_sum = jnp.sum(weights, axis=1)
    numerator = jnp.dot(weights.astype(jnp.bfloat16), values, preferred_element_type=jnp.float32)
    return (row_top, weight_sum, numerator)


def body(
    new_query,
    new_key,
    new_value,
    cache_keys,
    cache_values,
    cache_length,
    dealing,
    out_weight,
    stretch_query,
    stretch_key,
    stretch_value,
    prior_keys,
    prior_values,
    stretch_start,
):
    head_size = cache_keys.shape[2]
    group_size = new_query.shape[1] // head_size
    local_dec = new_query.shape[0]
    seq_rank = lax.axis_index("seq")
    seq_count = lax.axis_size("seq")
    total_dec = local_dec * seq_count
    every_query, every_key, every_value = (
        lax.all_gather(new_query, "seq", axis=0, tiled=True),
        lax.all_gather(new_key, "seq", axis=0, tiled=True),
        lax.all_gather(new_value, "seq", axis=0, tiled=True),
    )
    slot_ids = seq_rank * local_dec + jnp.arange(local_dec, dtype=jnp.int32)
    arrival_ids = jnp.arange(total_dec, dtype=jnp.int32)
    sources = jnp.sum(
        jnp.where(dealing[None, :] == slot_ids[:, None], arrival_ids[None, :], 0), axis=1
    )
    home_query = jnp.take(every_query, sources, axis=0)
    home_key = jnp.take(every_key, sources, axis=0)
    home_value = jnp.take(every_value, sources, axis=0)
    cache_span = cache_keys.shape[1]
    cache_pos = jnp.arange(cache_span, dtype=jnp.int32)

    def decode_slot(query_row, own_key, own_value, cached_keys, cached_values, length):
        key_all = jnp.concatenate([cached_keys, own_key[None, :]], axis=0)
        value_all = jnp.concatenate([cached_values, own_value[None, :]], axis=0)
        visible = jnp.concatenate([cache_pos < length, jnp.ones((1,), dtype=jnp.bool_)])
        visible = jnp.broadcast_to(visible[None, :], (group_size, cache_span + 1))
        row_top, weight_sum, numerator = partial_attend(
            query_row.reshape(group_size, head_size), key_all, value_all, visible
        )
        return (
            (numerator / weight_sum[:, None]).astype(jnp.bfloat16).reshape(group_size * head_size)
        )

    home_out = jax.vmap(decode_slot)(
        home_query, home_key, home_value, cache_keys, cache_values, cache_length
    )
    stored_terms = jnp.dot(
        lax.all_gather(home_out, "seq", axis=0, tiled=True),
        out_weight,
        preferred_element_type=jnp.float32,
    )
    arrival_terms = jnp.take(stored_terms, dealing, axis=0)
    decode_mixed = lax.psum_scatter(arrival_terms, "tp", scatter_dimension=0, tiled=True).astype(
        jnp.bfloat16
    )
    stretch_count, local_tok, _ = stretch_query.shape
    stretch_len = local_tok * seq_count
    prior_span = prior_keys.shape[1]
    row_count = stretch_len * group_size
    every_stretch_key, every_stretch_value = (
        lax.all_gather(stretch_key, "seq", axis=1, tiled=True),
        lax.all_gather(stretch_value, "seq", axis=1, tiled=True),
    )
    gathered_query = lax.all_gather(stretch_query, "seq", axis=1, tiled=True)
    prior_pos = seq_rank * prior_span + jnp.arange(prior_span, dtype=jnp.int32)
    peak_list, total_list, numer_list = ([], [], [])
    for stretch_index in range(stretch_count):
        queries_all = gathered_query[stretch_index].reshape(row_count, head_size)
        prior_visible = jnp.broadcast_to(
            (prior_pos < stretch_start[stretch_index])[None, :], (row_count, prior_span)
        )

        def work_part():
            return partial_attend(
                queries_all, prior_keys[stretch_index], prior_values[stretch_index], prior_visible
            )

        def skip_part():
            return (
                jnp.full((row_count,), NEG_FILL, jnp.float32),
                jnp.zeros((row_count,), jnp.float32),
                jnp.zeros((row_count, head_size), jnp.float32),
            )

        pieces = lax.cond(
            seq_rank * prior_span < stretch_start[stretch_index], work_part, skip_part
        )
        peak_list.append(pieces[0].reshape(stretch_len, group_size))
        total_list.append(pieces[1].reshape(stretch_len, group_size))
        numer_list.append(pieces[2].reshape(stretch_len, group_size, head_size))
    part_top = jnp.stack(peak_list)
    part_sum = jnp.stack(total_list)
    part_num = jnp.stack(numer_list)
    peak_all = lax.pmax(part_top, "seq")
    factor = jnp.exp(part_top - peak_all)
    got_sum, got_num = (
        lax.psum_scatter(part_sum * factor, "seq", scatter_dimension=1, tiled=True),
        lax.psum_scatter(part_num * factor[..., None], "seq", scatter_dimension=1, tiled=True),
    )
    got_top = lax.dynamic_slice_in_dim(peak_all, seq_rank * local_tok, local_tok, 1)
    local_rows = local_tok * group_size
    stretch_pos = jnp.arange(stretch_len, dtype=jnp.int32)
    own_token = seq_rank * local_tok + jnp.arange(local_rows, dtype=jnp.int32) // group_size
    causal = stretch_pos[None, :] <= own_token[:, None]
    self_tops, self_totals, self_numers = ([], [], [])
    for stretch_index in range(stretch_count):
        local_queries = stretch_query[stretch_index].reshape(local_rows, head_size)
        pieces = partial_attend(
            local_queries,
            every_stretch_key[stretch_index],
            every_stretch_value[stretch_index],
            causal,
        )
        self_tops.append(pieces[0].reshape(local_tok, group_size))
        self_totals.append(pieces[1].reshape(local_tok, group_size))
        self_numers.append(pieces[2].reshape(local_tok, group_size, head_size))
    self_top = jnp.stack(self_tops)
    final_top = jnp.maximum(got_top, self_top)
    first_factor = jnp.exp(got_top - final_top)
    second_factor = jnp.exp(self_top - final_top)
    got_sum = got_sum * first_factor + jnp.stack(self_totals) * second_factor
    got_num = got_num * first_factor[..., None] + jnp.stack(self_numers) * second_factor[..., None]
    stretch_out = (
        (got_num / got_sum[..., None])
        .astype(jnp.bfloat16)
        .reshape(stretch_count, local_tok, group_size * head_size)
    )
    return (decode_mixed, stretch_out)


def solution(mesh):
    return jax.shard_map(
        body,
        mesh=mesh,
        in_specs=(
            P("seq", "tp"),
            P("seq", "tp"),
            P("seq", "tp"),
            P("seq", None, "tp"),
            P("seq", None, "tp"),
            P("seq"),
            P(),
            P("tp", "seq"),
            P(None, "seq", "tp"),
            P(None, "seq", "tp"),
            P(None, "seq", "tp"),
            P(None, "seq", "tp"),
            P(None, "seq", "tp"),
            P(),
        ),
        out_specs=(P("tp", "seq"), P(None, "seq", "tp")),
        check_vma=False,
    )
```

profile of v0, /device:TPU:0, one launch (start us, length us, event | category | flops | bytes accessed | tf_op | source)
XLA Modules:
  0.0 355.2 jit_solution(8637244430150871322)
XLA Ops:
  7.2 0.7 all-gather.6.cloned.1.call-update
  8.0 1.4 fusion.85
  11.4 43.9 %all-gather.6.cloned.1.call-done = bf16[3,256,896]{2,1,0:T(8,128)(2,1)} async-done(((bf16[3,32,896]{2,1,0:T(8,128)(2,1)}), bf16[3,256,896]{2,1,0:T(8,128)(2,1)}) %all-gather.6.cloned.1.call-update) | async-done | bytes 1376272 | tf_op jit(solution)/shard_map/all_gather | solution.py:91
  55.3 21.5 %conditional.3 = (f32[1,256,7,128]{3,1,2,0:T(8,128)S(1)}, f32[1,256,7]{1,2,0:T(8,128)S(1)}, f32[1,256,7]{1,2,0:T(8,128)S(1)}) conditional(s32[]{:T(128)} %convert_element_type.44, () %tuple.51, (bf16[3,1024,128]{2,1,0:T(8,128)(2,1)}, bf16[3,256,896]{2,1,0:T(8,128)(2,1)}, s32[1024]{0:T(1024)S(1)}, bf16[3,1024,128]{2,1,0:T(8,128)(2,1)}, s32[]{:T(128)}) %tuple.52), branch_computations={%region_4.6_spmd, %region_5.9_spmd} | conditional | flops 956036608 | bytes 33706012 | solution.py:112
  55.3 0.6 broadcast_compare_fusion
  55.9 1.1 slice.81
  57.4 2.2 fusion
  59.6 3.8 %fusion.2 = (f32[1792]{0:T(1024)S(1)}, bf16[1792,1024]{1,0:T(8,128)(2,1)}) fusion(f32[1792,1024]{1,0:T(8,128)S(1)} %get-tuple-element.123, f32[1792]{0:T(1024)S(1)} %get-tuple-element.122, pred[1024]{0:T(1024)(128)(4,1)S(1)} %broadcast_compare_fusion), kind=kLoop, calls=%fused_computation.5 | loop fusion | flops 11008256 | bytes 11025408 | tf_op jit(solution)/shard_map/cond/branch_1_fun/reduce_sum | solution.py:16
  63.5 6.4 %reshape.159 = bf16[256,7,1024]{2,1,0:T(8,128)(2,1)} reshape(bf16[1792,1024]{1,0:T(8,128)(2,1)} %get-tuple-element.121) | data formatting | bytes 7340032 | tf_op jit(solution)/shard_map/reshape.122
  69.9 6.3 %fusion.5 = f32[1,256,7,128]{3,1,2,0:T(8,128)S(1)} fusion(bf16[256,7,1024]{2,1,0:T(8,128)(2,1)} %reshape.159, bf16[3,1024,128]{2,1,0:T(8,128)(2,1)} %get-tuple-element.37), kind=kOutput, calls=%fused_computation.8 | convolution fusion | flops 469762048 | bytes 5373952 | tf_op jit(solution)/shard_map/cond/branch_1_fun/dot_general | solution.py:17
  76.8 0.6 copy-done.3
  77.4 21.5 %conditional.4 = (f32[1,256,7,128]{3,1,2,0:T(8,128)S(1)}, f32[1,256,7]{1,2,0:T(8,128)S(1)}, f32[1,256,7]{1,2,0:T(8,128)S(1)}) conditional(s32[]{:T(128)} %convert_element_type.45, () %tuple.53, (bf16[3,1024,128]{2,1,0:T(8,128)(2,1)}, bf16[3,256,896]{2,1,0:T(8,128)(2,1)}, s32[1024]{0:T(1024)S(1)}, bf16[3,1024,128]{2,1,0:T(8,128)(2,1)}, ...), branch_computations={%region_8.10_spmd, %region_9.13_spmd} | conditional | flops 956036608 | bytes 33706012 | solution.py:112
  77.4 0.6 broadcast_compare_fusion.1
  78.1 1.1 slice.82
  79.6 2.2 fusion.13
  81.8 3.9 %fusion.15 = (f32[1792]{0:T(1024)S(1)}, bf16[1792,1024]{1,0:T(8,128)(2,1)}) fusion(f32[1792,1024]{1,0:T(8,128)S(1)} %get-tuple-element.127, f32[1792]{0:T(1024)S(1)} %get-tuple-element.126, pred[1024]{0:T(1024)(128)(4,1)S(1)} %broadcast_compare_fusion.1), kind=kLoop, calls=%fused_computation.19 | loop fusion | flops 11008256 | bytes 11025408 | tf_op jit(solution)/shard_map/cond/branch_1_fun/reduce_sum | solution.py:16
  85.6 6.4 %reshape.160 = bf16[256,7,1024]{2,1,0:T(8,128)(2,1)} reshape(bf16[1792,1024]{1,0:T(8,128)(2,1)} %get-tuple-element.125) | data formatting | bytes 7340032 | tf_op jit(solution)/shard_map/reshape.125
  92.1 6.3 %fusion.18 = f32[1,256,7,128]{3,1,2,0:T(8,128)S(1)} fusion(bf16[256,7,1024]{2,1,0:T(8,128)(2,1)} %reshape.160, bf16[3,1024,128]{2,1,0:T(8,128)(2,1)} %get-tuple-element.41), kind=kOutput, calls=%fused_computation.22 | convolution fusion | flops 469762048 | bytes 5373952 | tf_op jit(solution)/shard_map/cond/branch_1_fun/dot_general | solution.py:17
  99.0 0.6 copy-done.4
  99.6 23.7 %conditional.5 = (f32[1,256,7,128]{3,1,2,0:T(8,128)}, f32[1,256,7]{1,2,0:T(8,128)}, f32[1,256,7]{1,2,0:T(8,128)S(1)}) conditional(s32[]{:T(128)} %convert_element_type.46, () %tuple.55, (bf16[3,1024,128]{2,1,0:T(8,128)(2,1)}, bf16[3,256,896]{2,1,0:T(8,128)(2,1)}, s32[1024]{0:T(1024)S(1)}, bf16[3,1024,128]{2,1,0:T(8,128)(2,1)}, s32[]{:T(128)}) %tuple.56), branch_computations={%region_12.14_spmd, %region_13.17_spmd} | conditional | flops 956036608 | bytes 33710136 | solution.py:112
  99.6 1.3 broadcast_compare_fusion.2
  100.8 1.1 slice.83
  102.4 2.2 fusion.26
  104.6 3.8 %fusion.28 = (f32[1792]{0:T(1024)S(1)}, bf16[1792,1024]{1,0:T(8,128)(2,1)}) fusion(f32[1792,1024]{1,0:T(8,128)S(1)} %get-tuple-element.131, f32[1792]{0:T(1024)S(1)} %get-tuple-element.130, pred[1024]{0:T(1024)(128)(4,1)S(1)} %copy-done.7), kind=kLoop, calls=%fused_computation.33 | loop fusion | flops 11008256 | bytes 11025408 | tf_op jit(solution)/shard_map/cond/branch_1_fun/reduce_sum | solution.py:16
  108.4 6.4 %reshape.161 = bf16[256,7,1024]{2,1,0:T(8,128)(2,1)} reshape(bf16[1792,1024]{1,0:T(8,128)(2,1)} %get-tuple-element.129) | data formatting | bytes 7340032 | tf_op jit(solution)/shard_map/reshape.128
  114.9 7.2 %fusion.31 = f32[1,256,7,128]{3,1,2,0:T(8,128)} fusion(bf16[256,7,1024]{2,1,0:T(8,128)(2,1)} %reshape.161, bf16[3,1024,128]{2,1,0:T(8,128)(2,1)} %get-tuple-element.45), kind=kOutput, calls=%fused_computation.36 | convolution fusion | flops 469762048 | bytes 5373952 | tf_op jit(solution)/shard_map/cond/branch_1_fun/dot_general | solution.py:17
  122.6 0.7 copy.87
  123.3 1.3 constant_dynamic-update-slice_fusion
  124.6 34.1 %pmax.7 = f32[3,256,7]{1,2,0:T(8,128)S(1)} all-reduce(f32[3,256,7]{1,2,0:T(8,128)} %constant_dynamic-update-slice_fusion), channel_id=1, replica_groups=mesh['seq'=8,'tp'=4] {'seq'}, use_global_device_ids=true, to_apply=%region_16.18 | all-reduce | flops 5376 | bytes 43008 | tf_op jit(solution)/shard_map/pmax | solution.py:121
  158.7 0.8 maximum_multiply_fusion.2
  159.4 1.0 copy.76
  160.5 1.9 reshape.268
  162.5 3.0 maximum_multiply_fusion
  165.9 30.6 %all_gather.26 = bf16[3,256,128]{2,1,0:T(8,128)(2,1)S(1)} all-gather(bf16[3,32,128]{2,1,0:T(8,128)(2,1)S(1)} %copy-done.5), channel_id=1, replica_groups=mesh['seq'=8,'tp'=4] {'seq'}, dimensions={1}, use_global_device_ids=true | all-gather | bytes 221184 | tf_op jit(solution)/shard_map/all_gather | solution.py:88
  199.0 0.6 compare_select_fusion
  201.6 16.2 %all-gather.1 = bf16[8,1,128]{2,1,0:T(2,128)(2,1)S(1)} all-gather(bf16[1,1,128]{2,1,0:T(2,128)(2,1)S(1)} %bitcast.128), channel_id=1, replica_groups=mesh['seq'=8,'tp'=4] {'seq'}, dimensions={0}, use_global_device_ids=true | all-gather | bytes 2304 | tf_op jit(solution)/shard_map/all_gather | solution.py:45
  218.5 18.1 %all-gather.2 = bf16[8,1,128]{2,1,0:T(2,128)(2,1)S(1)} all-gather(bf16[1,1,128]{2,1,0:T(2,128)(2,1)S(1)} %bitcast.129), channel_id=1, replica_groups=mesh['seq'=8,'tp'=4] {'seq'}, dimensions={0}, use_global_device_ids=true | all-gather | bytes 2304 | tf_op jit(solution)/shard_map/all_gather | solution.py:46
  236.6 30.7 %all-gather = bf16[8,1,896]{2,1,0:T(2,128)(2,1)S(1)} all-gather(bf16[1,1,896]{2,1,0:T(2,128)(2,1)S(1)} %bitcast.125), channel_id=1, replica_groups=mesh['seq'=8,'tp'=4] {'seq'}, dimensions={0}, use_global_device_ids=true | all-gather | bytes 16128 | tf_op jit(solution)/shard_map/all_gather | solution.py:44
  267.5 1.7 fusion.86
  269.5 1.5 fusion.43
  271.0 30.4 %all-gather.3 = bf16[8,1,896]{2,1,0:T(2,128)(2,1)S(1)} all-gather(bf16[1,1,896]{2,1,0:T(2,128)(2,1)S(1)} %reshape.252), channel_id=1, replica_groups=mesh['seq'=8,'tp'=4] {'seq'}, dimensions={0}, use_global_device_ids=true | all-gather | bytes 16128 | tf_op jit(solution)/shard_map/all_gather | solution.py:75
  301.8 0.6 gather_fusion
  302.4 0.6 dynamic-slice.12
  303.7 10.1 %all-reduce = bf16[8,448]{1,0:T(8,128)(2,1)S(1)} all-reduce(f32[8,448]{1,0:T(8,128)S(1)} %broadcast_select_fusion), channel_id=2, replica_groups=mesh['seq'=8,'tp'=4] {'tp'}, use_global_device_ids=true, to_apply=%region_3.5.clone | all-reduce | flops 3584 | bytes 21504
  313.9 30.6 %all_gather.27 = bf16[3,256,128]{2,1,0:T(8,128)(2,1)S(1)} all-gather(bf16[3,32,128]{2,1,0:T(8,128)(2,1)S(1)} %copy-done.6), channel_id=1, replica_groups=mesh['seq'=8,'tp'=4] {'seq'}, dimensions={1}, use_global_device_ids=true | all-gather | bytes 221184 | tf_op jit(solution)/shard_map/all_gather | solution.py:89
  344.5 0.6 dynamic-slice_convert_fusion
  345.6 0.8 reshape.269
  346.6 2.0 copy_bitcast_fusion
  (90 shorter events, 7.4 us)
Async XLA Ops:
  7.2 294.3 %copy-start = (bf16[896,448]{0,1:T(8,128)(2,1)S(1)}, bf16[896,448]{0,1:T(8,128)(2,1)}, u32[]{:S(2)}) copy-start(bf16[896,448]{0,1:T(8,128)(2,1)} %param.29) | copy-start | bytes 2408452
  7.2 48.1 %all-gather.6.cloned.1.call-start = ((), (), s32[]{:S(2)}) async-start(), calls=%async_computation.2 | async-start | bytes 1548288 | tf_op jit(solution)/shard_map/all_gather | solution.py:91
  7.9 337.7 %reduce-scatter.7.cloned.1.call-start = ((), (), s32[]{:S(2)}) async-start(), calls=%async_computation.4 | async-start | bytes 147456
  76.8 0.6 copy-start.3
  98.9 0.6 copy-start.4
  98.9 0.6 copy-start.2
  102.3 2.2 copy-start.7
  162.4 3.2 copy-start.1
  162.4 184.2 %reduce-scatter.5.cloned.1.call-start = ((), (), s32[]{:S(2)}) async-start(), calls=%async_computation.3 | async-start | bytes 3096576 | tf_op jit(solution)/shard_map/reduce_scatter | solution.py:125
  162.4 3.4 copy-start.5
  165.5 33.5 %copy-start.11 = (s32[8]{0:T(128)S(1)}, s32[8]{0:T(128)}, u32[]{:S(2)}) copy-start(s32[8]{0:T(128)} %param.28) | copy-start | bytes 100
  165.5 36.1 %copy-start.9 = (bf16[1,128]{1,0:T(2,128)(2,1)S(1)}, bf16[1,128]{1,0:T(2,128)(2,1)}, u32[]{:S(2)}) copy-start(bf16[1,128]{1,0:T(2,128)(2,1)} %param.23) | copy-start | bytes 772
  165.5 53.0 %copy-start.10 = (bf16[1,128]{1,0:T(2,128)(2,1)S(1)}, bf16[1,128]{1,0:T(2,128)(2,1)}, u32[]{:S(2)}) copy-start(bf16[1,128]{1,0:T(2,128)(2,1)} %param.24) | copy-start | bytes 772
  165.5 71.1 %copy-start.8 = (bf16[1,896]{1,0:T(2,128)(2,1)S(1)}, bf16[1,896]{1,0:T(2,128)(2,1)}, u32[]{:S(2)}) copy-start(bf16[1,896]{1,0:T(2,128)(2,1)} %param.22) | copy-start | bytes 5380
  165.6 136.8 %copy-start.12 = (u32[32]{0:T(128)S(1)}, u32[32]{0:T(128)}, u32[]{:S(2)}) copy-start(u32[32]{0:T(128)} %constant.174) | copy-start | bytes 388
  165.7 148.2 %copy-start.6 = (bf16[3,32,128]{2,1,0:T(8,128)(2,1)S(1)}, bf16[3,32,128]{2,1,0:T(8,128)(2,1)}, u32[]{:S(2)}) copy-start(bf16[3,32,128]{2,1,0:T(8,128)(2,1)} %param.32) | copy-start | bytes 73732
Sparse Core Ops, SparseCore 0:
  10.2 45.0 all-gather.5
  162.5 58.1 reduce-scatter.6
  224.3 70.5 reduce-scatter.4
where the time goes:
time: 357 us; the launch traced here: 355 us
  blocking collectives  201 us (56%)
  waiting for transfers between devices  44.6 us (12%)
  local copies, waits for them, and re-layouts  37.3 us (10%)
  matrix products  31.3 us (9%)
  other arithmetic  21.5 us (6%)
  between operations  19.3 us (5%)
    all_gather x1, waiting for transfers between devices, body(): gathered_query = lax.all_gather(stretch_query, 'seq', axis=1, tiled=True)  43.9 us
    pmax x1, blocking collectives, body(): peak_all = lax.pmax(part_top, 'seq')  34.1 us
    all_gather x1, blocking collectives, body(): lax.all_gather(new_query, 'seq', axis=0, tiled=True)  30.7 us
    all_gather x1, blocking collectives, body(): lax.all_gather(stretch_key, 'seq', axis=1, tiled=True)  30.6 us
    all_gather x1, blocking collectives, body(): lax.all_gather(stretch_value, 'seq', axis=1, tiled=True)  30.6 us
    all_gather x1, blocking collectives, body(): lax.all_gather(home_out, 'seq', axis=0, tiled=True)  30.4 us
    dot_general x7, matrix products, partial_attend(): jnp.dot(weights.astype(jnp.bfloat16), values, preferred_element_type=jnp....  21.8 us
    another operation x6, local copies, waits for them, and re-layouts  19.5 us
  transfers between devices with their start and end apart: 3, of which 1 were waited for; matrix products, arithmetic and copies ran while one was open for 4% of the time, Pallas kernels for 0%

commit v1 on v0

--- a/solution.py
+++ b/solution.py
@@ -88,7 +88,12 @@
         lax.all_gather(stretch_key, "seq", axis=1, tiled=True),
         lax.all_gather(stretch_value, "seq", axis=1, tiled=True),
     )
-    gathered_query = lax.all_gather(stretch_query, "seq", axis=1, tiled=True)
+    ring = [stretch_query]
+    for hop in range(7):
+        ring.append(lax.ppermute(ring[-1], "seq", [(dev, (dev + 1) % 8) for dev in range(8)]))
+    gathered_query = jnp.roll(
+        jnp.concatenate(ring[::-1], axis=1), (lax.axis_index("seq") + 1) * ring[0].shape[1], axis=1
+    )
     prior_pos = seq_rank * prior_span + jnp.arange(prior_span, dtype=jnp.int32)
     peak_list, total_list, numer_list = ([], [], [])
     for stretch_index in range(stretch_count):

time: 357 us -> 374 us (1.048)
  waiting for transfers between devices: 44.6 us -> 54 us
    ppermute x0 -> x7, waiting for transfers between devices: none -> 53.9 us  [body(): lax.ppermute(ring[-1], 'seq', [(dev, (dev + 1) % 8) for dev in range(8)])]
    all_gather x1 -> x0, waiting for transfers between devices: 43.9 us -> none  [body(): gathered_query = lax.all_gather(stretch_query, 'seq', axis=1, tiled=True)]
  transfers between devices with their start and end apart: 3 -> 9, of which waited for: 1 -> 7; matrix products, arithmetic and copies ran while one was open for 4% -> 4% of each run, Pallas kernels for 0% -> 0%
where the time goes in v1:
time: 374 us; the launch traced here: 373 us
  blocking collectives  200 us (53%)
  waiting for transfers between devices  54 us (14%)
  local copies, waits for them, and re-layouts  40.8 us (11%)
  matrix products  31.1 us (8%)
  other arithmetic  23.6 us (6%)
  between operations  19.7 us (5%)
    ppermute x7, waiting for transfers between devices, body(): lax.ppermute(ring[-1], 'seq', [(dev, (dev + 1) % 8) for dev in range(8)])  53.9 us
    pmax x1, blocking collectives, body(): peak_all = lax.pmax(part_top, 'seq')  33.6 us
    all_gather x1, blocking collectives, body(): lax.all_gather(stretch_key, 'seq', axis=1, tiled=True)  30.7 us
    all_gather x1, blocking collectives, body(): lax.all_gather(stretch_value, 'seq', axis=1, tiled=True)  30.6 us
    all_gather x1, blocking collectives, body(): lax.all_gather(home_out, 'seq', axis=0, tiled=True)  30.5 us
    all_gather x1, blocking collectives, body(): lax.all_gather(new_query, 'seq', axis=0, tiled=True)  30.5 us
    dot_general x7, matrix products, partial_attend(): jnp.dot(weights.astype(jnp.bfloat16), values, preferred_element_type=jnp....  22.9 us
    another operation x6, local copies, waits for them, and re-layouts  19.5 us
  transfers between devices with their start and end apart: 9, of which 7 were waited for; matrix products, arithmetic and copies ran while one was open for 4% of the time, Pallas kernels for 0%

profile of v1, /device:TPU:0, one launch (start us, length us, event | category | flops | bytes accessed | tf_op | source)
XLA Modules:
  0.0 372.9 jit_solution(5981373588750178979)
XLA Ops:
  7.2 3.0 collective-permute-start
  10.3 7.6 %collective-permute-done = bf16[3,32,896]{2,1,0:T(8,128)(2,1)S(1)} collective-permute-done((bf16[3,32,896]{2,1,0:T(8,128)(2,1)}, bf16[3,32,896]{2,1,0:T(8,128)(2,1)S(1)}, u32[]{:S(2)}, u32[]{:S(2)}) %collective-permute-start) | collective-permute-done | bytes 172064 | tf_op jit(solution)/shard_map/ppermute | solution.py:93
  17.9 8.3 %collective-permute-done.1 = bf16[3,32,896]{2,1,0:T(8,128)(2,1)S(1)} collective-permute-done((bf16[3,32,896]{2,1,0:T(8,128)(2,1)S(1)}, bf16[3,32,896]{2,1,0:T(8,128)(2,1)S(1)}, u32[]{:S(2)}, u32[]{:S(2)}) %collective-permute-start.1) | collective-permute-done | bytes 172064 | tf_op jit(solution)/shard_map/ppermute | solution.py:93
  26.1 8.1 %collective-permute-done.2 = bf16[3,32,896]{2,1,0:T(8,128)(2,1)S(1)} collective-permute-done((bf16[3,32,896]{2,1,0:T(8,128)(2,1)S(1)}, bf16[3,32,896]{2,1,0:T(8,128)(2,1)S(1)}, u32[]{:S(2)}, u32[]{:S(2)}) %collective-permute-start.2) | collective-permute-done | bytes 172064 | tf_op jit(solution)/shard_map/ppermute | solution.py:93
  34.2 8.1 %collective-permute-done.3 = bf16[3,32,896]{2,1,0:T(8,128)(2,1)S(1)} collective-permute-done((bf16[3,32,896]{2,1,0:T(8,128)(2,1)S(1)}, bf16[3,32,896]{2,1,0:T(8,128)(2,1)S(1)}, u32[]{:S(2)}, u32[]{:S(2)}) %collective-permute-start.3) | collective-permute-done | bytes 172064 | tf_op jit(solution)/shard_map/ppermute | solution.py:93
  42.4 8.1 %collective-permute-done.4 = bf16[3,32,896]{2,1,0:T(8,128)(2,1)S(1)} collective-permute-done((bf16[3,32,896]{2,1,0:T(8,128)(2,1)S(1)}, bf16[3,32,896]{2,1,0:T(8,128)(2,1)S(1)}, u32[]{:S(2)}, u32[]{:S(2)}) %collective-permute-start.4) | collective-permute-done | bytes 172064 | tf_op jit(solution)/shard_map/ppermute | solution.py:93
  50.5 9.1 %collective-permute-done.5 = bf16[3,32,896]{2,1,0:T(8,128)(2,1)S(1)} collective-permute-done((bf16[3,32,896]{2,1,0:T(8,128)(2,1)S(1)}, bf16[3,32,896]{2,1,0:T(8,128)(2,1)S(1)}, u32[]{:S(2)}, u32[]{:S(2)}) %collective-permute-start.5) | collective-permute-done | bytes 172064 | tf_op jit(solution)/shard_map/ppermute | solution.py:93
  59.5 1.4 fusion.85
  63.0 4.7 %collective-permute-done.6 = bf16[3,32,896]{2,1,0:T(8,128)(2,1)S(1)} collective-permute-done((bf16[3,32,896]{2,1,0:T(8,128)(2,1)S(1)}, bf16[3,32,896]{2,1,0:T(8,128)(2,1)S(1)}, u32[]{:S(2)}, u32[]{:S(2)}) %collective-permute-start.6) | collective-permute-done | bytes 172064 | tf_op jit(solution)/shard_map/ppermute | solution.py:93
  67.8 0.9 constant_dynamic-update-slice_fusion.8
  69.1 21.8 %conditional.3 = (f32[1,256,7,128]{3,1,2,0:T(8,128)S(1)}, f32[1,256,7]{1,2,0:T(8,128)}, f32[1,256,7]{1,2,0:T(8,128)}) conditional(s32[]{:T(128)} %convert_element_type.44, () %tuple.51, (bf16[3,1024,128]{2,1,0:T(8,128)(2,1)}, bf16[3,256,896]{2,1,0:T(8,128)(2,1)S(1)}, s32[1024]{0:T(1024)S(1)}, bf16[3,1024,128]{2,1,0:T(8,128)(2,1)}, s32[]{:T(128)}) %tuple.52), branch_computations={%region_4.6_spmd, %region_5.9_spmd} | conditional | flops 956036608 | bytes 33763412 | solution.py:117
  70.3 2.2 fusion
  72.5 3.8 %fusion.2 = (f32[1792]{0:T(1024)S(1)}, bf16[1792,1024]{1,0:T(8,128)(2,1)}) fusion(f32[1792,1024]{1,0:T(8,128)S(1)} %get-tuple-element.123, f32[1792]{0:T(1024)S(1)} %get-tuple-element.122, pred[1024]{0:T(1024)(128)(4,1)S(1)} %broadcast_compare_fusion), kind=kLoop, calls=%fused_computation.5 | loop fusion | flops 11008256 | bytes 11025408 | tf_op jit(solution)/shard_map/cond/branch_1_fun/reduce_sum | solution.py:16
  76.4 6.4 %reshape.159 = bf16[256,7,1024]{2,1,0:T(8,128)(2,1)} reshape(bf16[1792,1024]{1,0:T(8,128)(2,1)} %get-tuple-element.121) | data formatting | bytes 7340032 | tf_op jit(solution)/shard_map/reshape.122
  82.8 6.3 %fusion.5 = f32[1,256,7,128]{3,1,2,0:T(8,128)S(1)} fusion(bf16[256,7,1024]{2,1,0:T(8,128)(2,1)} %reshape.159, bf16[3,1024,128]{2,1,0:T(8,128)(2,1)} %get-tuple-element.37), kind=kOutput, calls=%fused_computation.8 | convolution fusion | flops 469762048 | bytes 5373952 | tf_op jit(solution)/shard_map/cond/branch_1_fun/dot_general | solution.py:17
  89.3 0.7 copy.81
  90.9 1.3 constant_dynamic-update-slice_fusion.18
  92.2 25.8 %conditional.4 = (f32[1,256,7,128]{3,1,2,0:T(8,128)}, f32[1,256,7]{1,2,0:T(8,128)}, f32[1,256,7]{1,2,0:T(8,128)}) conditional(s32[]{:T(128)} %convert_element_type.45, () %tuple.53, (bf16[3,1024,128]{2,1,0:T(8,128)(2,1)}, bf16[3,256,896]{2,1,0:T(8,128)(2,1)S(1)}, s32[1024]{0:T(1024)}, bf16[3,1024,128]{2,1,0:T(8,128)(2,1)}, s32[]{:T(128)}) %tuple.113), branch_computations={%region_8.10_spmd, %region_9.13_spmd} | conditional | flops 956036608 | bytes 33767536 | solution.py:117
  92.2 1.9 broadcast_compare_fusion.1
  94.1 0.8 slice.82
  94.9 1.5 reshape_squeeze.25
  96.4 2.2 fusion.13
  98.7 3.8 %fusion.15 = (f32[1792]{0:T(1024)S(1)}, bf16[1792,1024]{1,0:T(8,128)(2,1)}) fusion(f32[1792,1024]{1,0:T(8,128)S(1)} %get-tuple-element.127, f32[1792]{0:T(1024)S(1)} %get-tuple-element.126, pred[1024]{0:T(1024)(128)(4,1)S(1)} %copy-done.10), kind=kLoop, calls=%fused_computation.19 | loop fusion | flops 11008256 | bytes 11025408 | tf_op jit(solution)/shard_map/cond/branch_1_fun/reduce_sum | solution.py:16
  102.5 6.4 %reshape.160 = bf16[256,7,1024]{2,1,0:T(8,128)(2,1)} reshape(bf16[1792,1024]{1,0:T(8,128)(2,1)} %get-tuple-element.125) | data formatting | bytes 7340032 | tf_op jit(solution)/shard_map/reshape.125
  109.0 7.3 %fusion.18 = f32[1,256,7,128]{3,1,2,0:T(8,128)} fusion(bf16[256,7,1024]{2,1,0:T(8,128)(2,1)} %reshape.160, bf16[3,1024,128]{2,1,0:T(8,128)(2,1)} %get-tuple-element.41), kind=kOutput, calls=%fused_computation.22 | convolution fusion | flops 469762048 | bytes 5373952 | tf_op jit(solution)/shard_map/cond/branch_1_fun/dot_general | solution.py:17
  118.0 1.3 constant_dynamic-update-slice_fusion.17
  119.3 23.9 %conditional.5 = (f32[1,256,7,128]{3,1,2,0:T(8,128)}, f32[1,256,7]{1,2,0:T(8,128)}, f32[1,256,7]{1,2,0:T(8,128)}) conditional(s32[]{:T(128)} %convert_element_type.46, () %tuple.55, (bf16[3,1024,128]{2,1,0:T(8,128)(2,1)}, bf16[3,256,896]{2,1,0:T(8,128)(2,1)S(1)}, s32[1024]{0:T(1024)}, bf16[3,1024,128]{2,1,0:T(8,128)(2,1)}, s32[]{:T(128)}) %tuple.114), branch_computations={%region_12.14_spmd, %region_13.17_spmd} | conditional | flops 956036608 | bytes 33710136 | solution.py:117
  119.3 1.9 broadcast_compare_fusion.2
  121.7 2.2 fusion.26
  124.0 3.8 %fusion.28 = (f32[1792]{0:T(1024)S(1)}, bf16[1792,1024]{1,0:T(8,128)(2,1)}) fusion(f32[1792,1024]{1,0:T(8,128)S(1)} %get-tuple-element.131, f32[1792]{0:T(1024)S(1)} %get-tuple-element.130, pred[1024]{0:T(1024)(128)(4,1)S(1)} %copy-done.11), kind=kLoop, calls=%fused_computation.33 | loop fusion | flops 11008256 | bytes 11025408 | tf_op jit(solution)/shard_map/cond/branch_1_fun/reduce_sum | solution.py:16
  127.8 6.4 %reshape.161 = bf16[256,7,1024]{2,1,0:T(8,128)(2,1)} reshape(bf16[1792,1024]{1,0:T(8,128)(2,1)} %get-tuple-element.129) | data formatting | bytes 7340032 | tf_op jit(solution)/shard_map/reshape.128
  134.2 7.2 %fusion.31 = f32[1,256,7,128]{3,1,2,0:T(8,128)} fusion(bf16[256,7,1024]{2,1,0:T(8,128)(2,1)} %reshape.161, bf16[3,1024,128]{2,1,0:T(8,128)(2,1)} %get-tuple-element.45), kind=kOutput, calls=%fused_computation.36 | convolution fusion | flops 469762048 | bytes 5373952 | tf_op jit(solution)/shard_map/cond/branch_1_fun/dot_general | solution.py:17
  143.2 1.3 constant_dynamic-update-slice_fusion.16
  144.5 33.6 %pmax.7 = f32[3,256,7]{1,2,0:T(8,128)S(1)} all-reduce(f32[3,256,7]{1,2,0:T(8,128)} %constant_dynamic-update-slice_fusion.16), channel_id=1, replica_groups=mesh['seq'=8,'tp'=4] {'seq'}, use_global_device_ids=true, to_apply=%region_16.18 | all-reduce | flops 5376 | bytes 43008 | tf_op jit(solution)/shard_map/pmax | solution.py:126
  178.1 0.8 maximum_multiply_fusion.2
  179.2 0.9 reshape.268
  180.2 3.2 maximum_multiply_fusion
  183.4 0.8 copy-done.2
  184.6 30.7 %all_gather.22 = bf16[3,256,128]{2,1,0:T(8,128)(2,1)S(1)} all-gather(bf16[3,32,128]{2,1,0:T(8,128)(2,1)S(1)} %copy-done.8), channel_id=1, replica_groups=mesh['seq'=8,'tp'=4] {'seq'}, dimensions={1}, use_global_device_ids=true | all-gather | bytes 221184 | tf_op jit(solution)/shard_map/all_gather | solution.py:88
  220.4 16.2 %all-gather.1 = bf16[8,1,128]{2,1,0:T(2,128)(2,1)S(1)} all-gather(bf16[1,1,128]{2,1,0:T(2,128)(2,1)S(1)} %bitcast.128), channel_id=1, replica_groups=mesh['seq'=8,'tp'=4] {'seq'}, dimensions={0}, use_global_device_ids=true | all-gather | bytes 2304 | tf_op jit(solution)/shard_map/all_gather | solution.py:45
  237.2 18.2 %all-gather.2 = bf16[8,1,128]{2,1,0:T(2,128)(2,1)S(1)} all-gather(bf16[1,1,128]{2,1,0:T(2,128)(2,1)S(1)} %bitcast.129), channel_id=1, replica_groups=mesh['seq'=8,'tp'=4] {'seq'}, dimensions={0}, use_global_device_ids=true | all-gather | bytes 2304 | tf_op jit(solution)/shard_map/all_gather | solution.py:46
  255.4 30.5 %all-gather = bf16[8,1,896]{2,1,0:T(2,128)(2,1)S(1)} all-gather(bf16[1,1,896]{2,1,0:T(2,128)(2,1)S(1)} %bitcast.125), channel_id=1, replica_groups=mesh['seq'=8,'tp'=4] {'seq'}, dimensions={0}, use_global_device_ids=true | all-gather | bytes 16128 | tf_op jit(solution)/shard_map/all_gather | solution.py:44
  286.8 1.5 fusion.43
  288.4 30.5 %all-gather.3 = bf16[8,1,896]{2,1,0:T(2,128)(2,1)S(1)} all-gather(bf16[1,1,896]{2,1,0:T(2,128)(2,1)S(1)} %reshape.252), channel_id=1, replica_groups=mesh['seq'=8,'tp'=4] {'seq'}, dimensions={0}, use_global_device_ids=true | all-gather | bytes 16128 | tf_op jit(solution)/shard_map/all_gather | solution.py:75
  321.2 10.1 %all-reduce = bf16[8,448]{1,0:T(8,128)(2,1)S(1)} all-reduce(f32[8,448]{1,0:T(8,128)S(1)} %broadcast_select_fusion), channel_id=2, replica_groups=mesh['seq'=8,'tp'=4] {'tp'}, use_global_device_ids=true, to_apply=%region_3.5.clone | all-reduce | flops 3584 | bytes 21504
  331.3 30.6 %all_gather.23 = bf16[3,256,128]{2,1,0:T(8,128)(2,1)S(1)} all-gather(bf16[3,32,128]{2,1,0:T(8,128)(2,1)S(1)} %copy-done.9), channel_id=1, replica_groups=mesh['seq'=8,'tp'=4] {'seq'}, dimensions={1}, use_global_device_ids=true | all-gather | bytes 221184 | tf_op jit(solution)/shard_map/all_gather | solution.py:89
  363.0 0.8 reshape.269
  364.1 2.0 copy_bitcast_fusion
  (128 shorter events, 14.3 us)
Async XLA Ops:
  7.2 311.7 %copy-start = (bf16[896,448]{0,1:T(8,128)(2,1)S(1)}, bf16[896,448]{0,1:T(8,128)(2,1)}, u32[]{:S(2)}) copy-start(bf16[896,448]{0,1:T(8,128)(2,1)} %param.29) | copy-start | bytes 2408452
  7.2 61.8 %copy-start.1 = (bf16[3,32,896]{2,1,0:T(8,128)(2,1)S(1)}, bf16[3,32,896]{2,1,0:T(8,128)(2,1)}, u32[]{:S(2)}) copy-start(bf16[3,32,896]{2,1,0:T(8,128)(2,1)} %param.30) | copy-start | bytes 516100
  7.2 355.8 %reduce-scatter.7.cloned.1.call-start = ((), (), s32[]{:S(2)}) async-start(), calls=%async_computation.3 | async-start | bytes 147456
  7.2 10.6 %collective-permute-start = (bf16[3,32,896]{2,1,0:T(8,128)(2,1)}, bf16[3,32,896]{2,1,0:T(8,128)(2,1)S(1)}, u32[]{:S(2)}, u32[]{:S(2)}) collective-permute-start(bf16[3,32,896]{2,1,0:T(8,128)(2,1)} %param.30), channel_id=1, source_target_pairs={{0,4},{4,8},{8,12},{12,16},{16,20},{20,24},{24,28},{28,0},{1,5},{5... | collective-permute-start | bytes 516104 | tf_op jit(solution)/shard_map/ppermute | solution.py:93
  17.9 8.3 %collective-permute-start.1 = (bf16[3,32,896]{2,1,0:T(8,128)(2,1)S(1)}, bf16[3,32,896]{2,1,0:T(8,128)(2,1)S(1)}, u32[]{:S(2)}, u32[]{:S(2)}) collective-permute-start(bf16[3,32,896]{2,1,0:T(8,128)(2,1)S(1)} %collective-permute-done), channel_id=1, source_target_pairs={{0,4},{4,8},{8,12},{12,16},{16,20},{20,24},{24,28},{28,0},{1,5},{5... | collective-permute-start | bytes 516104 | tf_op jit(solution)/shard_map/ppermute | solution.py:93
  26.1 8.1 %collective-permute-start.2 = (bf16[3,32,896]{2,1,0:T(8,128)(2,1)S(1)}, bf16[3,32,896]{2,1,0:T(8,128)(2,1)S(1)}, u32[]{:S(2)}, u32[]{:S(2)}) collective-permute-start(bf16[3,32,896]{2,1,0:T(8,128)(2,1)S(1)} %collective-permute-done.1), channel_id=1, source_target_pairs={{0,4},{4,8},{8,12},{12,16},{16,20},{20,24},{24,28},{28,0},{1,5},{5... | collective-permute-start | bytes 516104 | tf_op jit(solution)/shard_map/ppermute | solution.py:93
  34.2 8.1 %collective-permute-start.3 = (bf16[3,32,896]{2,1,0:T(8,128)(2,1)S(1)}, bf16[3,32,896]{2,1,0:T(8,128)(2,1)S(1)}, u32[]{:S(2)}, u32[]{:S(2)}) collective-permute-start(bf16[3,32,896]{2,1,0:T(8,128)(2,1)S(1)} %collective-permute-done.2), channel_id=1, source_target_pairs={{0,4},{4,8},{8,12},{12,16},{16,20},{20,24},{24,28},{28,0},{1,5},{5... | collective-permute-start | bytes 516104 | tf_op jit(solution)/shard_map/ppermute | solution.py:93
  42.3 8.1 %collective-permute-start.4 = (bf16[3,32,896]{2,1,0:T(8,128)(2,1)S(1)}, bf16[3,32,896]{2,1,0:T(8,128)(2,1)S(1)}, u32[]{:S(2)}, u32[]{:S(2)}) collective-permute-start(bf16[3,32,896]{2,1,0:T(8,128)(2,1)S(1)} %collective-permute-done.3), channel_id=1, source_target_pairs={{0,4},{4,8},{8,12},{12,16},{16,20},{20,24},{24,28},{28,0},{1,5},{5... | collective-permute-start | bytes 516104 | tf_op jit(solution)/shard_map/ppermute | solution.py:93
  50.5 9.1 %collective-permute-start.5 = (bf16[3,32,896]{2,1,0:T(8,128)(2,1)S(1)}, bf16[3,32,896]{2,1,0:T(8,128)(2,1)S(1)}, u32[]{:S(2)}, u32[]{:S(2)}) collective-permute-start(bf16[3,32,896]{2,1,0:T(8,128)(2,1)S(1)} %collective-permute-done.4), channel_id=1, source_target_pairs={{0,4},{4,8},{8,12},{12,16},{16,20},{20,24},{24,28},{28,0},{1,5},{5... | collective-permute-start | bytes 516104 | tf_op jit(solution)/shard_map/ppermute | solution.py:93
  59.5 8.1 %collective-permute-start.6 = (bf16[3,32,896]{2,1,0:T(8,128)(2,1)S(1)}, bf16[3,32,896]{2,1,0:T(8,128)(2,1)S(1)}, u32[]{:S(2)}, u32[]{:S(2)}) collective-permute-start(bf16[3,32,896]{2,1,0:T(8,128)(2,1)S(1)} %collective-permute-done.5), channel_id=1, source_target_pairs={{0,4},{4,8},{8,12},{12,16},{16,20},{20,24},{24,28},{28,0},{1,5},{5... | collective-permute-start | bytes 516104 | tf_op jit(solution)/shard_map/ppermute | solution.py:93
  63.0 6.2 %copy-start.7 = (s32[1024]{0:T(1024)}, s32[1024]{0:T(1024)S(1)}, u32[]{:S(2)}) copy-start(s32[1024]{0:T(1024)S(1)} %iota_add_fusion) | copy-start | bytes 12292
  72.5 3.9 %copy-start.3 = (f32[1792]{0:T(1024)}, f32[1792]{0:T(1024)S(1)}, u32[]{:S(2)}) copy-start(f32[1792]{0:T(1024)S(1)} %get-tuple-element.122) | copy-start | bytes 21508 | tf_op jit(solution)/shard_map/cond
  82.8 7.2 %copy-start.4 = (f32[1792]{0:T(1024)S(1)}, f32[1792]{0:T(1024)}, u32[]{:S(2)}) copy-start(f32[1792]{0:T(1024)} %copy-done.3) | copy-start | bytes 21508 | tf_op jit(solution)/shard_map/cond
  96.4 2.2 copy-start.10
  98.6 3.9 %copy-start.5 = (f32[1792]{0:T(1024)}, f32[1792]{0:T(1024)S(1)}, u32[]{:S(2)}) copy-start(f32[1792]{0:T(1024)S(1)} %get-tuple-element.126) | copy-start | bytes 21508 | tf_op jit(solution)/shard_map/cond
  109.0 8.2 %copy-start.6 = (f32[1792]{0:T(1024)S(1)}, f32[1792]{0:T(1024)}, u32[]{:S(2)}) copy-start(f32[1792]{0:T(1024)} %copy-done.5) | copy-start | bytes 21508 | tf_op jit(solution)/shard_map/cond
  121.7 2.2 copy-start.11
  180.1 183.9 %reduce-scatter.5.cloned.1.call-start = ((), (), s32[]{:S(2)}) async-start(), calls=%async_computation.2 | async-start | bytes 3096576 | tf_op jit(solution)/shard_map/reduce_scatter | solution.py:130
  183.3 0.9 copy-start.2
  183.3 1.2 copy-start.8
  183.4 34.4 %copy-start.15 = (s32[8]{0:T(128)S(1)}, s32[8]{0:T(128)}, u32[]{:S(2)}) copy-start(s32[8]{0:T(128)} %param.28) | copy-start | bytes 100
  183.4 37.0 %copy-start.13 = (bf16[1,128]{1,0:T(2,128)(2,1)S(1)}, bf16[1,128]{1,0:T(2,128)(2,1)}, u32[]{:S(2)}) copy-start(bf16[1,128]{1,0:T(2,128)(2,1)} %param.23) | copy-start | bytes 772
  183.4 53.8 %copy-start.14 = (bf16[1,128]{1,0:T(2,128)(2,1)S(1)}, bf16[1,128]{1,0:T(2,128)(2,1)}, u32[]{:S(2)}) copy-start(bf16[1,128]{1,0:T(2,128)(2,1)} %param.24) | copy-start | bytes 772
  183.4 72.0 %copy-start.12 = (bf16[1,896]{1,0:T(2,128)(2,1)S(1)}, bf16[1,896]{1,0:T(2,128)(2,1)}, u32[]{:S(2)}) copy-start(bf16[1,896]{1,0:T(2,128)(2,1)} %param.22) | copy-start | bytes 5380
  183.4 102.7 %copy-start.16 = (bf16[1,4096,128]{2,1,0:T(8,128)(2,1)S(1)}, bf16[1,4096,128]{2,1,0:T(8,128)(2,1)}, u32[]{:S(2)}) copy-start(bf16[1,4096,128]{2,1,0:T(8,128)(2,1)} %param.25) | copy-start | bytes 3145732
  217.1 102.7 %copy-start.17 = (u32[32]{0:T(128)S(1)}, u32[32]{0:T(128)}, u32[]{:S(2)}) copy-start(u32[32]{0:T(128)} %constant.195) | copy-start | bytes 388
  217.4 113.8 %copy-start.9 = (bf16[3,32,128]{2,1,0:T(8,128)(2,1)S(1)}, bf16[3,32,128]{2,1,0:T(8,128)(2,1)}, u32[]{:S(2)}) copy-start(bf16[3,32,128]{2,1,0:T(8,128)(2,1)} %param.32) | copy-start | bytes 73732
Sparse Core Ops, SparseCore 0:
  180.2 58.4 reduce-scatter.6
  242.3 70.6 reduce-scatter.4
